TPU v7x, 256 devices: a whole 4x4x8 slice. The times are simulated.
256 devices in a mesh: ctx: 32 (over y, z), tp: 8 (over x, core).
Axes of the slice: x: 4, y: 4, z: 8, core: 2. Of those that a mesh axis runs over, the one named last changes fastest.
Arguments:
- tokens: bfloat16 [16384, 4096], P('ctx', 'tp'), may hold values from -6 to 6
- qkv_blocks: bfloat16 [3, 4, 1024, 1024], P(None, None, None, 'tp'), may hold values from -0.046875 to 0.046875
- out_blocks: bfloat16 [4, 1024, 1024], P(None, 'tp'), may hold values from -0.046875 to 0.046875
- mix_factors: float32 [4, 4, 4, 4], replicated, may hold values from -4 to 4
- head_gain: float32 [4, 1024], P(None, 'tp'), may hold values from 0.1 to 1.9
Outputs:
- layer_out: bfloat16 [16384, 4096], P('ctx', 'tp')
All inputs are finite; a program needn't handle non-finite values.
Results may differ from a plain program's by a relative error of at most 0.025.
Values may be sent and summed in bfloat16 or wider, within the bound.
No kernel may reach another device: no remote copies, remote signals or barrier semaphores. Data moves between devices by JAX's collectives and lax.ppermute only.
A program may use at most 128 MiB of HBM per device.

v0:
```python
import functools
import jax
import jax.numpy as jnp
from jax import lax
from jax.sharding import PartitionSpec as P

PHM = 4
SPAN = 128
HEAD = 128
BLOCK = 1024
epsilon = 1e-06


def ring_gather(value, axis, devices, size, stride):
    here = lax.axis_index(axis)
    slots = [value]
    for shift in range(1, size):
        pairs = []
        for i in range(devices):
            k = i // stride % size
            pairs.append((i, i + ((k + shift) % size - k) * stride))
        slots.append(lax.ppermute(value, axis, pairs))
    source = (here // stride % size - jnp.arange(size)) % size
    return (jnp.stack(slots).astype(jnp.float32), source)


def exclusive_prefix(value, axis, devices, row):
    here = lax.axis_index(axis)
    pos, col = (here % row, here // row)
    within, source = ring_gather(value.astype(jnp.bfloat16), axis, devices, row, 1)
    before = jnp.einsum("k,k...->...", (source < pos).astype(jnp.float32), within)
    row_total = jnp.sum(within, axis=0)
    cols = devices // row
    across, source = ring_gather(row_total.astype(jnp.bfloat16), axis, devices, cols, row)
    return before + jnp.einsum("k,k...->...", (source < col).astype(jnp.float32), across)


def fold_weights(blocks, mixing):
    terms, rows, cols = blocks.shape
    folded = None
    for term_index in range(terms):
        part = (
            mixing[term_index][:, None, :, None]
            * blocks[term_index].astype(jnp.float32)[None, :, None, :]
        )
        folded = part if folded is None else folded + part
    return folded.astype(jnp.bfloat16).reshape(PHM * rows, PHM * cols)


def on_device(ctx_devices, ctx_row, tokens, qkv_blocks, out_blocks, mix_factors, head_gain):
    col_width = qkv_blocks.shape[-1]
    w_qkv = jnp.concatenate([fold_weights(qkv_blocks[p], mix_factors[p]) for p in range(3)], axis=1)
    w_out = fold_weights(out_blocks, mix_factors[3])
    whole = lax.all_gather(tokens, "tp", axis=1, tiled=True)
    tok_rows = whole.shape[0]
    local_heads = PHM * col_width // HEAD
    nblk = tok_rows // SPAN
    qkv = jnp.dot(whole, w_qkv, preferred_element_type=jnp.float32).astype(jnp.bfloat16)

    def project(p):
        part = qkv[:, p * PHM * col_width : (p + 1) * PHM * col_width]
        return part.reshape(nblk, SPAN, local_heads, HEAD)

    key_heads = project(1)
    value_heads = project(2)
    states = jnp.einsum(
        "nshd,nshe->nhde", key_heads, value_heads, preferred_element_type=jnp.float32
    )
    totals = jnp.sum(states, axis=0)
    earlier_sum = exclusive_prefix(totals, "ctx", ctx_devices, ctx_row)
    query_heads = project(0)
    scores = jnp.einsum(
        "nshd,nthd->nhst", query_heads, key_heads, preferred_element_type=jnp.float32
    )
    causal = jnp.arange(SPAN)[:, None] >= jnp.arange(SPAN)[None, :]
    scores = jnp.where(causal[None, None], scores, 0.0).astype(jnp.bfloat16)
    within = jnp.einsum("nhst,nthe->nshe", scores, value_heads, preferred_element_type=jnp.float32)
    prefixes = [earlier_sum]
    for n in range(1, nblk):
        prefixes.append(prefixes[-1] + states[n - 1])
    prefix = jnp.stack(prefixes, axis=0)
    prefix_hi = prefix.astype(jnp.bfloat16)
    prefix_lo = (prefix - prefix_hi.astype(jnp.float32)).astype(jnp.bfloat16)
    carried_out = jnp.einsum(
        "nshd,nhde->nshe", query_heads, prefix_hi, preferred_element_type=jnp.float32
    ) + jnp.einsum("nshd,nhde->nshe", query_heads, prefix_lo, preferred_element_type=jnp.float32)
    combined = within + carried_out
    mean_sq = jnp.mean(combined * combined, axis=-1, keepdims=True)
    normed = combined * lax.rsqrt(mean_sq + epsilon) * head_gain
    attn = normed.astype(jnp.bfloat16).reshape(tok_rows, PHM * col_width)
    partial_value = jnp.dot(attn, w_out, preferred_element_type=jnp.float32)
    reduced = lax.psum_scatter(
        partial_value.astype(jnp.bfloat16), "tp", scatter_dimension=1, tiled=True
    )
    return reduced


def ctx_row_of(mesh):
    n = mesh.shape["ctx"]
    return 8 if n % 8 == 0 else n


def solution(mesh):
    placed = (P("ctx", "tp"), P(None, None, None, "tp"), P(None, "tp", None), P(), P(None, "tp"))
    return jax.shard_map(
        functools.partial(on_device, mesh.shape["ctx"], ctx_row_of(mesh)),
        mesh=mesh,
        in_specs=placed,
        out_specs=P("ctx", "tp"),
        check_vma=False,
    )
```

profile of v0, /device:TPU:8, one launch (start us, length us, event | category | flops | bytes accessed | tf_op | source)
XLA Modules:
  0.0 160.8 jit_solution(9527223819864626604)
XLA Ops:
  6.5 0.0 all-gather.2.cloned.1.call-start
  6.5 0.7 all-gather.2.cloned.1.call-update
  7.3 0.0 reduce-scatter.2.cloned.1.call-start
  7.3 0.9 slice_bitcast_fusion.18
  8.2 2.2 %bitcast_convert_fusion.15 = (f32[1024,128]{1,0:T(8,128)S(1)}, f32[1024,128]{1,0:T(8,128)S(1)}, f32[1024,128]{1,0:T(8,128)S(1)}, f32[1024,128]{1,0:T(8,128)S(1)}...) fusion(bf16[3,4,1024,128]{3,2,1,0:T(8,128)(2,1)} %param.6), kind=kLoop, calls=%fused_computation.62 | loop fusion | flops 1572864 | bytes 9437184 | tf_op jit(solution)/shard_map/convert_element_type | solution.py:44
  10.4 9.1 %add_convert_fusion.1 = (bf16[4,1024,4,128]{3,2,1,0:T(4,128)(2,1)S(1)}, bf16[4,1024,4,128]{3,2,1,0:T(4,128)(2,1)S(1)}) fusion(f32[1024,128]{1,0:T(8,128)S(1)} %get-tuple-element.17, f32[4,4]{1,0:T(4,128)S(1)} %get-tuple-element.30, f32[1024,128]{1,0:T(8,128)S(1)} %get-tuple-element.18, f32[4,4]{1,0:T(4,128)S(1)} %get-tuple-element.31, ...), kind=kLoop, calls=%fused_computation.7 | loop fusion | flops 33554432 | bytes 12583424 | tf_op jit(solution)/shard_map/convert.17
  19.6 2.7 %copy.52 = bf16[512,8,4,128]{3,1,2,0:T(8,128)(2,1)} copy(bf16[512,8,4,128]{3,2,1,0:T(4,128)(2,1)S(1)} %bitcast.181) | data formatting | bytes 8388608
  22.2 2.6 %copy.53 = bf16[512,8,4,128]{3,1,2,0:T(8,128)(2,1)} copy(bf16[512,8,4,128]{3,2,1,0:T(4,128)(2,1)S(1)} %bitcast.180) | data formatting | bytes 8388608
  24.9 4.6 %add_convert_fusion.3 = bf16[4,1024,4,128]{3,2,1,0:T(4,128)(2,1)S(1)} fusion(f32[1024,128]{1,0:T(8,128)S(1)} %get-tuple-element.14, f32[4,4]{1,0:T(4,128)S(1)} %get-tuple-element.38, f32[1024,128]{1,0:T(8,128)S(1)} %get-tuple-element.15, f32[4,4]{1,0:T(4,128)S(1)} %get-tuple-element.39, f32[1024,128]{1,0:T(8,128)S(1)} %get-tuple-element.16, ...), kind=kLoop, calls=%fused_computation.9 | loop fusion | flops 16777216 | bytes 6291712 | tf_op jit(solution)/shard_map/convert.19
  29.5 0.0 copy-start.1
  29.5 2.7 %copy.54 = bf16[512,8,4,128]{3,1,2,0:T(8,128)(2,1)} copy(bf16[512,8,4,128]{3,2,1,0:T(4,128)(2,1)S(1)} %bitcast.182) | data formatting | bytes 8388608
  32.2 0.0 copy-done.1
  32.2 0.2 bitcast_convert_fusion.3
  32.4 4.8 %add_convert_fusion = bf16[4,128,4,1024]{3,2,1,0:T(4,128)(2,1)S(1)} fusion(f32[128,1024]{1,0:T(8,128)S(1)} %get-tuple-element.24, f32[4,4]{1,0:T(4,128)S(1)} %get-tuple-element.41, f32[128,1024]{1,0:T(8,128)S(1)} %get-tuple-element.25, f32[4,4]{1,0:T(4,128)S(1)} %get-tuple-element.42, f32[128,1024]{1,0:T(8,128)S(1)} %get-tuple-element.23, ...), kind=kLoop, calls=%fused_computation.6 | loop fusion | flops 16777216 | bytes 6291712 | tf_op jit(solution)/shard_map/convert_element_type | solution.py:47
  37.3 4.2 %copy.33 = bf16[64,8,4,1024]{3,1,2,0:T(8,128)(2,1)} copy(bf16[64,8,4,1024]{3,2,1,0:T(4,128)(2,1)S(1)} %bitcast.183) | data formatting | bytes 8388608
  41.5 5.1 %all-gather.2.cloned.1.call-done = bf16[512,4096]{1,0:T(8,128)(2,1)} async-done(((bf16[512,512]{1,0:T(8,128)(2,1)}), bf16[512,4096]{1,0:T(8,128)(2,1)}) %all-gather.2.cloned.1.call-update) | async-done | bytes 4194320 | tf_op jit(solution)/shard_map/all_gather | solution.py:54
  46.7 13.8 %fusion.9 = bf16[512,1536]{0,1:T(8,128)(2,1)} fusion(bf16[512,4096]{1,0:T(8,128)(2,1)} %all-gather.2.cloned.1.call-done, bf16[4096,512]{1,0:T(8,128)(2,1)} %bitcast.187, bf16[4096,512]{1,0:T(8,128)(2,1)} %bitcast.188, bf16[4096,512]{1,0:T(8,128)(2,1)} %bitcast.189), kind=kOutput, calls=%fused_computation.15 | convolution fusion | flops 6480986112 | bytes 18350080 | tf_op jit(solution)/shard_map/dot_general | solution.py:58
  60.5 1.5 fusion.65
  61.9 0.1 reshape.328
  62.1 0.4 copy.15
  62.4 0.1 reshape.330
  62.6 0.3 fusion.66
  62.9 1.6 %collective-permute-start = (bf16[4,128,128]{2,1,0:T(8,128)(2,1)S(1)}, bf16[4,128,128]{2,1,0:T(8,128)(2,1)S(1)}, u32[]{:S(2)}, u32[]{:S(2)}) collective-permute-start(bf16[4,128,128]{2,1,0:T(8,128)(2,1)S(1)} %get-tuple-element.43), channel_id=1, source_target_pairs={{0,8},{8,16},{16,24},{24,32},{32,40},{40,48},{48,56},{56,0},{64,72... | collective-permute-start | bytes 393224 | tf_op jit(solution)/shard_map/ppermute | solution.py:22
  64.5 2.5 %collective-permute-start.1 = (bf16[4,128,128]{2,1,0:T(8,128)(2,1)S(1)}, bf16[4,128,128]{2,1,0:T(8,128)(2,1)S(1)}, u32[]{:S(2)}, u32[]{:S(2)}) collective-permute-start(bf16[4,128,128]{2,1,0:T(8,128)(2,1)S(1)} %get-tuple-element.43), channel_id=1, source_target_pairs={{0,16},{8,24},{16,32},{24,40},{32,48},{40,56},{48,0},{56,8},{64,80... | collective-permute-start | bytes 393224 | tf_op jit(solution)/shard_map/ppermute | solution.py:22
  67.1 2.9 %collective-permute-start.2 = (bf16[4,128,128]{2,1,0:T(8,128)(2,1)S(1)}, bf16[4,128,128]{2,1,0:T(8,128)(2,1)}, u32[]{:S(2)}, u32[]{:S(2)}) collective-permute-start(bf16[4,128,128]{2,1,0:T(8,128)(2,1)S(1)} %get-tuple-element.43), channel_id=1, source_target_pairs={{0,24},{8,32},{16,40},{24,48},{32,56},{40,0},{48,8},{56,16},{64,88... | collective-permute-start | bytes 393224 | tf_op jit(solution)/shard_map/ppermute | solution.py:22
  70.0 2.0 %collective-permute-start.3 = (bf16[4,128,128]{2,1,0:T(8,128)(2,1)S(1)}, bf16[4,128,128]{2,1,0:T(8,128)(2,1)}, u32[]{:S(2)}, u32[]{:S(2)}) collective-permute-start(bf16[4,128,128]{2,1,0:T(8,128)(2,1)S(1)} %get-tuple-element.43), channel_id=1, source_target_pairs={{0,32},{8,40},{16,48},{24,56},{32,0},{40,8},{48,16},{56,24},{64,96... | collective-permute-start | bytes 393224 | tf_op jit(solution)/shard_map/ppermute | solution.py:22
  72.0 3.1 %collective-permute-start.4 = (bf16[4,128,128]{2,1,0:T(8,128)(2,1)S(1)}, bf16[4,128,128]{2,1,0:T(8,128)(2,1)}, u32[]{:S(2)}, u32[]{:S(2)}) collective-permute-start(bf16[4,128,128]{2,1,0:T(8,128)(2,1)S(1)} %get-tuple-element.43), channel_id=1, source_target_pairs={{0,40},{8,48},{16,56},{24,0},{32,8},{40,16},{48,24},{56,32},{64,10... | collective-permute-start | bytes 393224 | tf_op jit(solution)/shard_map/ppermute | solution.py:22
  75.1 0.1 reshape.329
  75.3 0.4 copy.17
  75.6 1.6 %fusion.15 = f32[4,4,128,128]{3,2,1,0:T(8,128)} fusion(bf16[4,128,4,128]{3,1,2,0:T(8,128)(2,1)S(1)} %copy.15, bf16[4,128,4,128]{3,1,2,0:T(8,128)(2,1)S(1)} %copy.17, pred[128,128]{1,0:T(8,128)(4,1)S(1)} %iota_compare_fusion, bf16[4,128,4,128]{1,0,3,2:T(4,128)(2,1)S(1)} %reshape.330), kind=kOutput, calls=%fused_computation.21 | convolution fusion | flops 134742016 | bytes 2637824 | tf_op jit(solution)/shard_map/nhst,nthe->nshe/dot_general | solution.py:77
  77.3 0.0 collective-permute-done
  77.3 3.4 %collective-permute-start.5 = (bf16[4,128,128]{2,1,0:T(8,128)(2,1)S(1)}, bf16[4,128,128]{2,1,0:T(8,128)(2,1)S(1)}, u32[]{:S(2)}, u32[]{:S(2)}) collective-permute-start(bf16[4,128,128]{2,1,0:T(8,128)(2,1)S(1)} %get-tuple-element.43), channel_id=1, source_target_pairs={{0,48},{8,56},{16,0},{24,8},{32,16},{40,24},{48,32},{56,40},{64,11... | collective-permute-start | bytes 393224 | tf_op jit(solution)/shard_map/ppermute | solution.py:22
  80.7 0.0 collective-permute-done.1
  80.7 1.4 collective-permute-start.6
  82.1 2.0 %collective-permute-done.2 = bf16[4,128,128]{2,1,0:T(8,128)(2,1)} collective-permute-done((bf16[4,128,128]{2,1,0:T(8,128)(2,1)S(1)}, bf16[4,128,128]{2,1,0:T(8,128)(2,1)}, u32[]{:S(2)}, u32[]{:S(2)}) %collective-permute-start.2) | collective-permute-done | bytes 131104 | tf_op jit(solution)/shard_map/ppermute | solution.py:22
  84.0 4.6 %collective-permute-done.3 = bf16[4,128,128]{2,1,0:T(8,128)(2,1)} collective-permute-done((bf16[4,128,128]{2,1,0:T(8,128)(2,1)S(1)}, bf16[4,128,128]{2,1,0:T(8,128)(2,1)}, u32[]{:S(2)}, u32[]{:S(2)}) %collective-permute-start.3) | collective-permute-done | bytes 131104 | tf_op jit(solution)/shard_map/ppermute | solution.py:22
  88.6 2.8 %collective-permute-done.4 = bf16[4,128,128]{2,1,0:T(8,128)(2,1)} collective-permute-done((bf16[4,128,128]{2,1,0:T(8,128)(2,1)S(1)}, bf16[4,128,128]{2,1,0:T(8,128)(2,1)}, u32[]{:S(2)}, u32[]{:S(2)}) %collective-permute-start.4) | collective-permute-done | bytes 131104 | tf_op jit(solution)/shard_map/ppermute | solution.py:22
  91.4 3.7 %collective-permute-done.5 = bf16[4,128,128]{2,1,0:T(8,128)(2,1)S(1)} collective-permute-done((bf16[4,128,128]{2,1,0:T(8,128)(2,1)S(1)}, bf16[4,128,128]{2,1,0:T(8,128)(2,1)S(1)}, u32[]{:S(2)}, u32[]{:S(2)}) %collective-permute-start.5) | collective-permute-done | bytes 131104 | tf_op jit(solution)/shard_map/ppermute | solution.py:22
  95.1 1.1 collective-permute-done.6
  96.2 1.1 add_add_fusion
  97.3 1.6 collective-permute-start.7
  98.8 1.1 collective-permute-start.8
  100.0 2.1 %collective-permute-start.9 = (bf16[4,128,128]{2,1,0:T(8,128)(2,1)S(1)}, bf16[4,128,128]{2,1,0:T(8,128)(2,1)S(1)}, u32[]{:S(2)}, u32[]{:S(2)}) collective-permute-start(bf16[4,128,128]{2,1,0:T(8,128)(2,1)S(1)} %add_add_fusion), channel_id=1, source_target_pairs={{0,192},{8,200},{16,208},{24,216},{32,224},{40,232},{48,240},{56,2... | collective-permute-start | bytes 393224 | tf_op jit(solution)/shard_map/ppermute | solution.py:22
  102.2 0.9 bitcast_dynamic-update-slice_fusion.4
  103.1 0.9 bitcast_dynamic-update-slice_fusion.3
  104.0 0.9 bitcast_dynamic-update-slice_fusion.2
  105.0 0.0 copy-start
  105.0 0.7 fusion.16
  105.8 0.0 collective-permute-done.7
  105.8 0.2 collective-permute-done.8
  106.0 0.6 collective-permute-done.9
  106.6 0.1 pad_maximum_fusion.1
  106.7 0.5 fusion.22
  107.2 0.1 fusion.36
  107.2 0.0 copy-start.2
  107.3 0.1 fusion.33
  107.3 0.5 fusion.30
  107.8 0.0 copy-done
  107.8 0.5 multiply_reduce_fusion
  108.4 0.2 multiply_convert_fusion
  108.6 0.3 copy.20
  108.9 6.5 %convolution_convert_fusion = bf16[512,4096]{1,0:T(8,128)(2,1)} fusion(bf16[512,4096]{1,0:T(8,128)(2,1)} %bitcast.186, bf16[64,8,4,128]{3,2,1,0:T(4,128)(2,1)S(1)} %bitcast.191), kind=kOutput, calls=%fused_computation.10 | convolution fusion | flops 2149580800 | bytes 8912896 | tf_op jit(solution)/shard_map/dot_general | solution.py:91
  115.4 0.0 reduce-scatter.2.cloned.1.call-update
  115.5 38.5 %reduce-scatter.2.cloned.1.call-done = bf16[512,512]{1,0:T(8,128)(2,1)} async-done(((bf16[512,4096]{1,0:T(8,128)(2,1)}), bf16[512,512]{1,0:T(8,128)(2,1)}) %reduce-scatter.2.cloned.1.call-update) | async-done | bytes 524304 | tf_op jit(solution)/shard_map/reduce_scatter | solution.py:92
  (8 shorter events, 0.1 us)
Async XLA Ops:
  6.5 40.1 %all-gather.2.cloned.1.call-start = ((), (), s32[]{:S(2)}) async-start(), calls=%async_computation.1 | async-start | bytes 4718592 | tf_op jit(solution)/shard_map/all_gather | solution.py:54
  7.3 146.7 %reduce-scatter.2.cloned.1.call-start = ((), (), s32[]{:S(2)}) async-start(), calls=%async_computation.2 | async-start | bytes 4718592 | tf_op jit(solution)/shard_map/reduce_scatter | solution.py:92
  29.5 2.7 %copy-start.1 = (bf16[4,128,1024]{2,1,0:T(8,128)(2,1)S(1)}, bf16[4,128,1024]{2,1,0:T(8,128)(2,1)}, u32[]{:S(2)}) copy-start(bf16[4,128,1024]{2,1,0:T(8,128)(2,1)} %param.7) | copy-start | bytes 3145732
  62.9 14.4 %collective-permute-start = (bf16[4,128,128]{2,1,0:T(8,128)(2,1)S(1)}, bf16[4,128,128]{2,1,0:T(8,128)(2,1)S(1)}, u32[]{:S(2)}, u32[]{:S(2)}) collective-permute-start(bf16[4,128,128]{2,1,0:T(8,128)(2,1)S(1)} %get-tuple-element.43), channel_id=1, source_target_pairs={{0,8},{8,16},{16,24},{24,32},{32,40},{40,48},{48,56},{56,0},{64,72... | collective-permute-start | bytes 393224 | tf_op jit(solution)/shard_map/ppermute | solution.py:22
  64.5 16.2 %collective-permute-start.1 = (bf16[4,128,128]{2,1,0:T(8,128)(2,1)S(1)}, bf16[4,128,128]{2,1,0:T(8,128)(2,1)S(1)}, u32[]{:S(2)}, u32[]{:S(2)}) collective-permute-start(bf16[4,128,128]{2,1,0:T(8,128)(2,1)S(1)} %get-tuple-element.43), channel_id=1, source_target_pairs={{0,16},{8,24},{16,32},{24,40},{32,48},{40,56},{48,0},{56,8},{64,80... | collective-permute-start | bytes 393224 | tf_op jit(solution)/shard_map/ppermute | solution.py:22
  67.1 17.0 %collective-permute-start.2 = (bf16[4,128,128]{2,1,0:T(8,128)(2,1)S(1)}, bf16[4,128,128]{2,1,0:T(8,128)(2,1)}, u32[]{:S(2)}, u32[]{:S(2)}) collective-permute-start(bf16[4,128,128]{2,1,0:T(8,128)(2,1)S(1)} %get-tuple-element.43), channel_id=1, source_target_pairs={{0,24},{8,32},{16,40},{24,48},{32,56},{40,0},{48,8},{56,16},{64,88... | collective-permute-start | bytes 393224 | tf_op jit(solution)/shard_map/ppermute | solution.py:22
  70.0 18.6 %collective-permute-start.3 = (bf16[4,128,128]{2,1,0:T(8,128)(2,1)S(1)}, bf16[4,128,128]{2,1,0:T(8,128)(2,1)}, u32[]{:S(2)}, u32[]{:S(2)}) collective-permute-start(bf16[4,128,128]{2,1,0:T(8,128)(2,1)S(1)} %get-tuple-element.43), channel_id=1, source_target_pairs={{0,32},{8,40},{16,48},{24,56},{32,0},{40,8},{48,16},{56,24},{64,96... | collective-permute-start | bytes 393224 | tf_op jit(solution)/shard_map/ppermute | solution.py:22
  72.0 19.4 %collective-permute-start.4 = (bf16[4,128,128]{2,1,0:T(8,128)(2,1)S(1)}, bf16[4,128,128]{2,1,0:T(8,128)(2,1)}, u32[]{:S(2)}, u32[]{:S(2)}) collective-permute-start(bf16[4,128,128]{2,1,0:T(8,128)(2,1)S(1)} %get-tuple-element.43), channel_id=1, source_target_pairs={{0,40},{8,48},{16,56},{24,0},{32,8},{40,16},{48,24},{56,32},{64,10... | collective-permute-start | bytes 393224 | tf_op jit(solution)/shard_map/ppermute | solution.py:22
  77.3 17.8 %collective-permute-start.5 = (bf16[4,128,128]{2,1,0:T(8,128)(2,1)S(1)}, bf16[4,128,128]{2,1,0:T(8,128)(2,1)S(1)}, u32[]{:S(2)}, u32[]{:S(2)}) collective-permute-start(bf16[4,128,128]{2,1,0:T(8,128)(2,1)S(1)} %get-tuple-element.43), channel_id=1, source_target_pairs={{0,48},{8,56},{16,0},{24,8},{32,16},{40,24},{48,32},{56,40},{64,11... | collective-permute-start | bytes 393224 | tf_op jit(solution)/shard_map/ppermute | solution.py:22
  80.7 15.5 %collective-permute-start.6 = (bf16[4,128,128]{2,1,0:T(8,128)(2,1)S(1)}, bf16[4,128,128]{2,1,0:T(8,128)(2,1)S(1)}, u32[]{:S(2)}, u32[]{:S(2)}) collective-permute-start(bf16[4,128,128]{2,1,0:T(8,128)(2,1)S(1)} %get-tuple-element.43), channel_id=1, source_target_pairs={{0,56},{8,0},{16,8},{24,16},{32,24},{40,32},{48,40},{56,48},{64,12... | collective-permute-start | bytes 393224 | tf_op jit(solution)/shard_map/ppermute | solution.py:22
  97.3 8.5 %collective-permute-start.7 = (bf16[4,128,128]{2,1,0:T(8,128)(2,1)S(1)}, bf16[4,128,128]{2,1,0:T(8,128)(2,1)S(1)}, u32[]{:S(2)}, u32[]{:S(2)}) collective-permute-start(bf16[4,128,128]{2,1,0:T(8,128)(2,1)S(1)} %add_add_fusion), channel_id=1, source_target_pairs={{0,64},{8,72},{16,80},{24,88},{32,96},{40,104},{48,112},{56,120},{... | collective-permute-start | bytes 393224 | tf_op jit(solution)/shard_map/ppermute | solution.py:22
  98.8 7.1 %collective-permute-start.8 = (bf16[4,128,128]{2,1,0:T(8,128)(2,1)S(1)}, bf16[4,128,128]{2,1,0:T(8,128)(2,1)S(1)}, u32[]{:S(2)}, u32[]{:S(2)}) collective-permute-start(bf16[4,128,128]{2,1,0:T(8,128)(2,1)S(1)} %add_add_fusion), channel_id=1, source_target_pairs={{0,128},{8,136},{16,144},{24,152},{32,160},{40,168},{48,176},{56,1... | collective-permute-start | bytes 393224 | tf_op jit(solution)/shard_map/ppermute | solution.py:22
  100.0 6.6 %collective-permute-start.9 = (bf16[4,128,128]{2,1,0:T(8,128)(2,1)S(1)}, bf16[4,128,128]{2,1,0:T(8,128)(2,1)S(1)}, u32[]{:S(2)}, u32[]{:S(2)}) collective-permute-start(bf16[4,128,128]{2,1,0:T(8,128)(2,1)S(1)} %add_add_fusion), channel_id=1, source_target_pairs={{0,192},{8,200},{16,208},{24,216},{32,224},{40,232},{48,240},{56,2... | collective-permute-start | bytes 393224 | tf_op jit(solution)/shard_map/ppermute | solution.py:22
  105.0 2.8 %copy-start = (f32[4,4,128,128]{3,2,1,0:T(8,128)S(1)}, f32[4,4,128,128]{3,2,1,0:T(8,128)}, u32[]{:S(2)}) copy-start(f32[4,4,128,128]{3,2,1,0:T(8,128)} %fusion.15) | copy-start | bytes 3145732
  107.2 1.2 copy-start.2
Sparse Core Ops, SparseCore 0:
  9.2 37.4 all-gather.1
  115.6 38.3 reduce-scatter.1
where the time goes:
time: 161 us
  waiting for transfers between devices  59.3 us (37%)
  matrix products  24.6 us (15%)
  other arithmetic  22.5 us (14%)
  starting transfers between devices  21.9 us (14%)
  local copies, waits for them, and re-layouts  18.9 us (12%)
  between operations  13.7 us (9%)
    reduce_scatter x1, waiting for transfers between devices, on_device(): lax.psum_scatter(partial_value.astype(jnp.bfloat16), 'tp', scatter_dimens...  38.5 us
    ppermute x10, starting transfers between devices, ring_gather(): slots.append(lax.ppermute(value, axis, pairs))  21.8 us
    unnamed x17, local copies, waits for them, and re-layouts  15.1 us
    ppermute x10, waiting for transfers between devices, ring_gather(): slots.append(lax.ppermute(value, axis, pairs))  15 us
    dot_general x1, matrix products, on_device(): jnp.dot(whole, w_qkv, preferred_element_type=jnp.float32)  13.8 us
    another operation x2, other arithmetic  13.7 us
    dot_general x1, matrix products, on_device(): partial_value = jnp.dot(attn, w_out, preferred_element_type=jnp.float32)  6.53 us
    all_gather x1, waiting for transfers between devices, on_device(): whole = lax.all_gather(tokens, 'tp', axis=1, tiled=True)  5.13 us
  transfers between devices with their start and end apart: 12, of which 9 were waited for; matrix products, arithmetic and copies ran while one was open for 25% of the time, Pallas kernels for 0%

commit v1 on v0

--- a/solution.py
+++ b/solution.py
@@ -9,6 +9,16 @@
 HEAD = 128
 BLOCK = 1024
 epsilon = 1e-06
+
+
+def get_the_chunk(m, peer_axis, dim_no):
+    reply = jnp.stack([m for _ in range(lax.axis_size(peer_axis))])
+    met_up = lax.all_to_all(reply, concat_axis=0, split_axis=0, axis_name=peer_axis)
+    prior = jnp.concatenate(met_up, dim_no)
+    return prior
+
+
+move_strips_all = functools.partial(get_the_chunk, peer_axis="tp", dim_no=1)
 
 
 def ring_gather(value, axis, devices, size, stride):
@@ -51,7 +61,7 @@
     col_width = qkv_blocks.shape[-1]
     w_qkv = jnp.concatenate([fold_weights(qkv_blocks[p], mix_factors[p]) for p in range(3)], axis=1)
     w_out = fold_weights(out_blocks, mix_factors[3])
-    whole = lax.all_gather(tokens, "tp", axis=1, tiled=True)
+    whole = move_strips_all(tokens)
     tok_rows = whole.shape[0]
     local_heads = PHM * col_width // HEAD
     nblk = tok_rows // SPAN

time: 161 us -> 178 us (1.11)
  starting transfers between devices: 21.9 us -> 30.8 us
  waiting for transfers between devices: 59.3 us -> 63.6 us
  local copies, waits for them, and re-layouts: 18.9 us -> 22.7 us
    all_to_all x0 -> x1, waiting for transfers between devices: none -> 13.1 us  [get_the_chunk(): lax.all_to_all(reply, concat_axis=0, split_axis=0, axis_name=peer_axis)]
    all_gather x1 -> x0, waiting for transfers between devices: 5.13 us -> none  [on_device(): whole = lax.all_gather(tokens, 'tp', axis=1, tiled=True)]
    all_to_all x0 -> x1, starting transfers between devices: none -> 4.83 us  [get_the_chunk(): lax.all_to_all(reply, concat_axis=0, split_axis=0, axis_name=peer_axis)]
    ppermute x10, starting transfers between devices: 21.8 us -> 25.9 us  [ring_gather(): slots.append(lax.ppermute(value, axis, pairs))]
    unnamed x17 -> x32, local copies, waits for them, and re-layouts: 15.1 us -> 18.8 us
    ppermute x10, waiting for transfers between devices: 15 us -> 12.6 us  [ring_gather(): slots.append(lax.ppermute(value, axis, pairs))]
    another operation x0 -> x1, local copies, waits for them, and re-layouts: none -> 2.36 us  [get_the_chunk(): reply = jnp.stack([m for _ in range(lax.axis_size(peer_axis))])]
  transfers between devices with their start and end apart: 12 -> 12, of which waited for: 9 -> 8; matrix products, arithmetic and copies ran while one was open for 25% -> 24% of each run, Pallas kernels for 0% -> 0%
where the time goes in v1:
time: 178 us; the launch traced here: 177 us
  waiting for transfers between devices  63.6 us (36%)
  starting transfers between devices  30.8 us (17%)
  matrix products  23.3 us (13%)
  other arithmetic  23.2 us (13%)
  local copies, waits for them, and re-layouts  22.7 us (13%)
  between operations  13.7 us (8%)
    reduce_scatter x1, waiting for transfers between devices, on_device(): lax.psum_scatter(partial_value.astype(jnp.bfloat16), 'tp', scatter_dimens...  37.9 us
    ppermute x10, starting transfers between devices, ring_gather(): slots.append(lax.ppermute(value, axis, pairs))  25.9 us
    unnamed x32, local copies, waits for them, and re-layouts  18.8 us
    another operation x2, other arithmetic  14.9 us
    all_to_all x1, waiting for transfers between devices, get_the_chunk(): lax.all_to_all(reply, concat_axis=0, split_axis=0, axis_name=peer_axis)  13.1 us
    ppermute x10, waiting for transfers between devices, ring_gather(): slots.append(lax.ppermute(value, axis, pairs))  12.6 us
    dot_general x1, matrix products, on_device(): jnp.dot(whole, w_qkv, preferred_element_type=jnp.float32)  12.6 us
    dot_general x1, matrix products, on_device(): partial_value = jnp.dot(attn, w_out, preferred_element_type=jnp.float32)  6.49 us
  transfers between devices with their start and end apart: 12, of which 8 were waited for; matrix products, arithmetic and copies ran while one was open for 24% of the time, Pallas kernels for 0%

profile of v1, /device:TPU:8, one launch (start us, length us, event | category | flops | bytes accessed | tf_op | source)
XLA Modules:
  0.0 177.3 jit_solution(12167838803466493151)
XLA Ops:
  6.5 1.3 copy.13
  7.8 2.4 %stack.66 = bf16[8,512,512]{1,2,0:T(8,128)(2,1)} broadcast(bf16[512,512]{0,1:T(8,128)(2,1)S(1)} %copy.13), dimensions={1,2} | broadcast | bytes 4718592 | tf_op jit(solution)/shard_map/stack | solution.py:15
  10.2 4.8 %all-to-all-start = ((bf16[8,512,512]{1,2,0:T(8,128)(2,1)}), bf16[8,512,512]{1,2,0:T(8,128)(2,1)}, u32[]{:S(2)}, u32[]{:S(2)}) async-start(bf16[8,512,512]{1,2,0:T(8,128)(2,1)} %stack.66), calls=%async_computation | async-start | bytes 8388608 | tf_op jit(solution)/shard_map/all_to_all | solution.py:16
  15.0 0.0 reduce-scatter.2.cloned.1.call-start
  15.0 0.0 copy-done.8
  15.1 0.0 copy-done.2
  15.1 1.7 bitcast_convert_fusion.15
  16.8 10.3 %add_convert_fusion.1 = (bf16[4,1024,4,128]{3,2,1,0:T(4,128)(2,1)}, bf16[4,1024,4,128]{3,2,1,0:T(4,128)(2,1)}) fusion(f32[1024,128]{1,0:T(8,128)S(1)} %get-tuple-element.17, f32[4,4]{1,0:T(4,128)S(1)} %get-tuple-element.30, f32[1024,128]{1,0:T(8,128)S(1)} %get-tuple-element.18, f32[4,4]{1,0:T(4,128)S(1)} %get-tuple-element.31, ...), kind=kLoop, calls=%fused_computation.7 | loop fusion | flops 33554432 | bytes 12583424 | tf_op jit(solution)/shard_map/convert.17
  27.1 5.0 %copy.53 = bf16[512,8,4,128]{3,1,2,0:T(8,128)(2,1)} copy(bf16[512,8,4,128]{3,2,1,0:T(4,128)(2,1)} %bitcast.184) | data formatting | bytes 8388608
  32.1 2.7 %copy.54 = bf16[512,8,4,128]{3,1,2,0:T(8,128)(2,1)} copy(bf16[512,8,4,128]{3,2,1,0:T(4,128)(2,1)S(1)} %bitcast.183) | data formatting | bytes 8388608
  34.8 4.6 %add_convert_fusion.3 = bf16[4,1024,4,128]{3,2,1,0:T(4,128)(2,1)S(1)} fusion(f32[1024,128]{1,0:T(8,128)S(1)} %copy-done.4, f32[4,4]{1,0:T(4,128)S(1)} %get-tuple-element.38, f32[1024,128]{1,0:T(8,128)S(1)} %copy-done.5, f32[4,4]{1,0:T(4,128)S(1)} %get-tuple-element.39, f32[1024,128]{1,0:T(8,128)S(1)} %copy-done.6, f32[4,4]{1,0:T(4,128)S(1)} %get-tuple-element.40, ...), kind=kLoop, calls=%fused_computation.9 | loop fusion | flops 16777216 | bytes 6291712 | tf_op jit(solution)/shard_map/convert.19
  39.4 0.0 copy-start.7
  39.5 2.7 %copy.55 = bf16[512,8,4,128]{3,1,2,0:T(8,128)(2,1)} copy(bf16[512,8,4,128]{3,2,1,0:T(4,128)(2,1)S(1)} %bitcast.185) | data formatting | bytes 8388608
  42.2 0.2 bitcast_convert_fusion.3
  42.4 4.8 %add_convert_fusion = bf16[4,128,4,1024]{3,2,1,0:T(4,128)(2,1)S(1)} fusion(f32[128,1024]{1,0:T(8,128)S(1)} %get-tuple-element.24, f32[4,4]{1,0:T(4,128)S(1)} %get-tuple-element.41, f32[128,1024]{1,0:T(8,128)S(1)} %get-tuple-element.25, f32[4,4]{1,0:T(4,128)S(1)} %get-tuple-element.42, f32[128,1024]{1,0:T(8,128)S(1)} %get-tuple-element.23, ...), kind=kLoop, calls=%fused_computation.6 | loop fusion | flops 16777216 | bytes 6291712 | tf_op jit(solution)/shard_map/convert_element_type | solution.py:57
  47.2 4.3 %copy.34 = bf16[64,8,4,1024]{3,1,2,0:T(8,128)(2,1)} copy(bf16[64,8,4,1024]{3,2,1,0:T(4,128)(2,1)S(1)} %bitcast.186) | data formatting | bytes 8388608
  51.5 13.1 %all-to-all-done = bf16[8,512,512]{1,2,0:T(8,128)(2,1)} async-done(((bf16[8,512,512]{1,2,0:T(8,128)(2,1)}), bf16[8,512,512]{1,2,0:T(8,128)(2,1)}, u32[]{:S(2)}, u32[]{:S(2)}) %all-to-all-start) | async-done | bytes 4194336 | tf_op jit(solution)/shard_map/all_to_all | solution.py:16
  64.6 12.6 %fusion.9 = bf16[512,1536]{0,1:T(8,128)(2,1)S(1)} fusion(bf16[512,4096]{0,1:T(8,128)(2,1)} %bitcast.25, bf16[4096,512]{1,0:T(8,128)(2,1)} %bitcast.190, bf16[4096,512]{1,0:T(8,128)(2,1)} %bitcast.191, bf16[4096,512]{1,0:T(8,128)(2,1)} %bitcast.192), kind=kOutput, calls=%fused_computation.15 | convolution fusion | flops 6480986112 | bytes 18350080 | tf_op jit(solution)/shard_map/dot_general | solution.py:68
  77.2 0.1 fusion.65
  77.3 0.1 reshape.338
  77.5 0.4 copy.16
  77.9 0.1 reshape.340
  78.0 0.3 fusion.66
  78.3 2.0 %collective-permute-start = (bf16[4,128,128]{2,1,0:T(8,128)(2,1)S(1)}, bf16[4,128,128]{2,1,0:T(8,128)(2,1)S(1)}, u32[]{:S(2)}, u32[]{:S(2)}) collective-permute-start(bf16[4,128,128]{2,1,0:T(8,128)(2,1)S(1)} %get-tuple-element.43), channel_id=1, source_target_pairs={{0,8},{8,16},{16,24},{24,32},{32,40},{40,48},{48,56},{56,0},{64,72... | collective-permute-start | bytes 393224 | tf_op jit(solution)/shard_map/ppermute | solution.py:32
  80.3 3.3 %collective-permute-start.1 = (bf16[4,128,128]{2,1,0:T(8,128)(2,1)S(1)}, bf16[4,128,128]{2,1,0:T(8,128)(2,1)S(1)}, u32[]{:S(2)}, u32[]{:S(2)}) collective-permute-start(bf16[4,128,128]{2,1,0:T(8,128)(2,1)S(1)} %get-tuple-element.43), channel_id=1, source_target_pairs={{0,16},{8,24},{16,32},{24,40},{32,48},{40,56},{48,0},{56,8},{64,80... | collective-permute-start | bytes 393224 | tf_op jit(solution)/shard_map/ppermute | solution.py:32
  83.6 4.0 %collective-permute-start.2 = (bf16[4,128,128]{2,1,0:T(8,128)(2,1)S(1)}, bf16[4,128,128]{2,1,0:T(8,128)(2,1)}, u32[]{:S(2)}, u32[]{:S(2)}) collective-permute-start(bf16[4,128,128]{2,1,0:T(8,128)(2,1)S(1)} %get-tuple-element.43), channel_id=1, source_target_pairs={{0,24},{8,32},{16,40},{24,48},{32,56},{40,0},{48,8},{56,16},{64,88... | collective-permute-start | bytes 393224 | tf_op jit(solution)/shard_map/ppermute | solution.py:32
  87.6 0.5 collective-permute-start.3
  88.1 5.0 %collective-permute-start.4 = (bf16[4,128,128]{2,1,0:T(8,128)(2,1)S(1)}, bf16[4,128,128]{2,1,0:T(8,128)(2,1)}, u32[]{:S(2)}, u32[]{:S(2)}) collective-permute-start(bf16[4,128,128]{2,1,0:T(8,128)(2,1)S(1)} %get-tuple-element.43), channel_id=1, source_target_pairs={{0,40},{8,48},{16,56},{24,0},{32,8},{40,16},{48,24},{56,32},{64,10... | collective-permute-start | bytes 393224 | tf_op jit(solution)/shard_map/ppermute | solution.py:32
  93.1 0.1 reshape.339
  93.2 0.4 copy.18
  93.6 1.7 fusion.15
  95.3 0.0 collective-permute-done
  95.3 2.7 %collective-permute-start.5 = (bf16[4,128,128]{2,1,0:T(8,128)(2,1)S(1)}, bf16[4,128,128]{2,1,0:T(8,128)(2,1)S(1)}, u32[]{:S(2)}, u32[]{:S(2)}) collective-permute-start(bf16[4,128,128]{2,1,0:T(8,128)(2,1)S(1)} %get-tuple-element.43), channel_id=1, source_target_pairs={{0,48},{8,56},{16,0},{24,8},{32,16},{40,24},{48,32},{56,40},{64,11... | collective-permute-start | bytes 393224 | tf_op jit(solution)/shard_map/ppermute | solution.py:32
  97.9 0.0 collective-permute-done.1
  97.9 3.4 %collective-permute-start.6 = (bf16[4,128,128]{2,1,0:T(8,128)(2,1)S(1)}, bf16[4,128,128]{2,1,0:T(8,128)(2,1)S(1)}, u32[]{:S(2)}, u32[]{:S(2)}) collective-permute-start(bf16[4,128,128]{2,1,0:T(8,128)(2,1)S(1)} %get-tuple-element.43), channel_id=1, source_target_pairs={{0,56},{8,0},{16,8},{24,16},{32,24},{40,32},{48,40},{56,48},{64,12... | collective-permute-start | bytes 393224 | tf_op jit(solution)/shard_map/ppermute | solution.py:32
  101.4 3.8 %collective-permute-done.2 = bf16[4,128,128]{2,1,0:T(8,128)(2,1)} collective-permute-done((bf16[4,128,128]{2,1,0:T(8,128)(2,1)S(1)}, bf16[4,128,128]{2,1,0:T(8,128)(2,1)}, u32[]{:S(2)}, u32[]{:S(2)}) %collective-permute-start.2) | collective-permute-done | bytes 131104 | tf_op jit(solution)/shard_map/ppermute | solution.py:32
  105.2 0.0 collective-permute-done.3
  105.2 3.8 %collective-permute-done.4 = bf16[4,128,128]{2,1,0:T(8,128)(2,1)} collective-permute-done((bf16[4,128,128]{2,1,0:T(8,128)(2,1)S(1)}, bf16[4,128,128]{2,1,0:T(8,128)(2,1)}, u32[]{:S(2)}, u32[]{:S(2)}) %collective-permute-start.4) | collective-permute-done | bytes 131104 | tf_op jit(solution)/shard_map/ppermute | solution.py:32
  109.0 2.1 %collective-permute-done.5 = bf16[4,128,128]{2,1,0:T(8,128)(2,1)S(1)} collective-permute-done((bf16[4,128,128]{2,1,0:T(8,128)(2,1)S(1)}, bf16[4,128,128]{2,1,0:T(8,128)(2,1)S(1)}, u32[]{:S(2)}, u32[]{:S(2)}) %collective-permute-start.5) | collective-permute-done | bytes 131104 | tf_op jit(solution)/shard_map/ppermute | solution.py:32
  111.1 1.5 collective-permute-done.6
  112.7 1.1 add_add_fusion
  113.7 1.7 collective-permute-start.7
  115.4 0.9 collective-permute-start.8
  116.3 2.4 %collective-permute-start.9 = (bf16[4,128,128]{2,1,0:T(8,128)(2,1)S(1)}, bf16[4,128,128]{2,1,0:T(8,128)(2,1)S(1)}, u32[]{:S(2)}, u32[]{:S(2)}) collective-permute-start(bf16[4,128,128]{2,1,0:T(8,128)(2,1)S(1)} %add_add_fusion), channel_id=1, source_target_pairs={{0,192},{8,200},{16,208},{24,216},{32,224},{40,232},{48,240},{56,2... | collective-permute-start | bytes 393224 | tf_op jit(solution)/shard_map/ppermute | solution.py:32
  118.8 0.9 bitcast_dynamic-update-slice_fusion.4
  119.7 0.9 bitcast_dynamic-update-slice_fusion.3
  120.7 0.9 bitcast_dynamic-update-slice_fusion.2
  121.6 0.7 fusion.16
  122.4 0.0 collective-permute-done.7
  122.4 0.6 collective-permute-done.8
  123.0 0.7 collective-permute-done.9
  123.7 0.1 pad_maximum_fusion.1
  123.8 0.5 fusion.22
  124.3 0.1 fusion.36
  124.4 0.0 copy-start.9
  124.4 0.1 fusion.33
  124.4 0.5 fusion.30
  125.0 0.0 copy-done.1
  125.0 0.5 multiply_reduce_fusion
  125.5 0.2 multiply_convert_fusion
  125.7 0.3 copy.21
  126.0 6.5 %convolution_convert_fusion = bf16[512,4096]{1,0:T(8,128)(2,1)} fusion(bf16[512,4096]{1,0:T(8,128)(2,1)} %bitcast.189, bf16[64,8,4,128]{3,2,1,0:T(4,128)(2,1)S(1)} %bitcast.194), kind=kOutput, calls=%fused_computation.10 | convolution fusion | flops 2149580800 | bytes 8912896 | tf_op jit(solution)/shard_map/dot_general | solution.py:101
  132.5 0.0 reduce-scatter.2.cloned.1.call-update
  132.6 37.9 %reduce-scatter.2.cloned.1.call-done = bf16[512,512]{1,0:T(8,128)(2,1)} async-done(((bf16[512,4096]{1,0:T(8,128)(2,1)}), bf16[512,512]{1,0:T(8,128)(2,1)}) %reduce-scatter.2.cloned.1.call-update) | async-done | bytes 524304 | tf_op jit(solution)/shard_map/reduce_scatter | solution.py:102
  (23 shorter events, 0.1 us)
Async XLA Ops:
  10.1 4.9 %copy-start.8 = (f32[4,4,4,4]{3,2,1,0:T(4,128)S(1)}, f32[4,4,4,4]{3,2,1,0:T(4,128)}, u32[]{:S(2)}) copy-start(f32[4,4,4,4]{3,2,1,0:T(4,128)} %param.8) | copy-start | bytes 3076
  10.2 4.9 %copy-start.2 = (bf16[3,4,1024,128]{3,2,1,0:T(8,128)(2,1)S(1)}, bf16[3,4,1024,128]{3,2,1,0:T(8,128)(2,1)}, u32[]{:S(2)}) copy-start(bf16[3,4,1024,128]{3,2,1,0:T(8,128)(2,1)} %param.6) | copy-start | bytes 9437188
  10.2 54.5 %all-to-all-start = ((bf16[8,512,512]{1,2,0:T(8,128)(2,1)}), bf16[8,512,512]{1,2,0:T(8,128)(2,1)}, u32[]{:S(2)}, u32[]{:S(2)}) async-start(bf16[8,512,512]{1,2,0:T(8,128)(2,1)} %stack.66), calls=%async_computation | async-start | bytes 8388608 | tf_op jit(solution)/shard_map/all_to_all | solution.py:16
  15.0 155.5 %reduce-scatter.2.cloned.1.call-start = ((), (), s32[]{:S(2)}) async-start(), calls=%async_computation.2 | async-start | bytes 4718592 | tf_op jit(solution)/shard_map/reduce_scatter | solution.py:102
  27.1 5.0 %copy-start = (bf16[4,1024,4,128]{3,2,1,0:T(4,128)(2,1)S(1)}, bf16[4,1024,4,128]{3,2,1,0:T(4,128)(2,1)}, u32[]{:S(2)}) copy-start(bf16[4,1024,4,128]{3,2,1,0:T(4,128)(2,1)} %get-tuple-element.48) | copy-start | bytes 12582916
  32.1 2.7 %copy-start.3 = (f32[1024,128]{1,0:T(8,128)S(1)}, f32[1024,128]{1,0:T(8,128)}, u32[]{:S(2)}) copy-start(f32[1024,128]{1,0:T(8,128)} %get-tuple-element.7) | copy-start | bytes 1572868
  32.1 2.7 %copy-start.4 = (f32[1024,128]{1,0:T(8,128)S(1)}, f32[1024,128]{1,0:T(8,128)}, u32[]{:S(2)}) copy-start(f32[1024,128]{1,0:T(8,128)} %get-tuple-element.14) | copy-start | bytes 1572868
  32.1 2.7 %copy-start.5 = (f32[1024,128]{1,0:T(8,128)S(1)}, f32[1024,128]{1,0:T(8,128)}, u32[]{:S(2)}) copy-start(f32[1024,128]{1,0:T(8,128)} %get-tuple-element.15) | copy-start | bytes 1572868
  32.1 2.7 %copy-start.6 = (f32[1024,128]{1,0:T(8,128)S(1)}, f32[1024,128]{1,0:T(8,128)}, u32[]{:S(2)}) copy-start(f32[1024,128]{1,0:T(8,128)} %get-tuple-element.16) | copy-start | bytes 1572868
  39.4 2.7 %copy-start.7 = (bf16[4,128,1024]{2,1,0:T(8,128)(2,1)S(1)}, bf16[4,128,1024]{2,1,0:T(8,128)(2,1)}, u32[]{:S(2)}) copy-start(bf16[4,128,1024]{2,1,0:T(8,128)(2,1)} %param.7) | copy-start | bytes 3145732
  78.3 17.0 %collective-permute-start = (bf16[4,128,128]{2,1,0:T(8,128)(2,1)S(1)}, bf16[4,128,128]{2,1,0:T(8,128)(2,1)S(1)}, u32[]{:S(2)}, u32[]{:S(2)}) collective-permute-start(bf16[4,128,128]{2,1,0:T(8,128)(2,1)S(1)} %get-tuple-element.43), channel_id=1, source_target_pairs={{0,8},{8,16},{16,24},{24,32},{32,40},{40,48},{48,56},{56,0},{64,72... | collective-permute-start | bytes 393224 | tf_op jit(solution)/shard_map/ppermute | solution.py:32
  80.3 17.6 %collective-permute-start.1 = (bf16[4,128,128]{2,1,0:T(8,128)(2,1)S(1)}, bf16[4,128,128]{2,1,0:T(8,128)(2,1)S(1)}, u32[]{:S(2)}, u32[]{:S(2)}) collective-permute-start(bf16[4,128,128]{2,1,0:T(8,128)(2,1)S(1)} %get-tuple-element.43), channel_id=1, source_target_pairs={{0,16},{8,24},{16,32},{24,40},{32,48},{40,56},{48,0},{56,8},{64,80... | collective-permute-start | bytes 393224 | tf_op jit(solution)/shard_map/ppermute | solution.py:32
  83.6 21.6 %collective-permute-start.2 = (bf16[4,128,128]{2,1,0:T(8,128)(2,1)S(1)}, bf16[4,128,128]{2,1,0:T(8,128)(2,1)}, u32[]{:S(2)}, u32[]{:S(2)}) collective-permute-start(bf16[4,128,128]{2,1,0:T(8,128)(2,1)S(1)} %get-tuple-element.43), channel_id=1, source_target_pairs={{0,24},{8,32},{16,40},{24,48},{32,56},{40,0},{48,8},{56,16},{64,88... | collective-permute-start | bytes 393224 | tf_op jit(solution)/shard_map/ppermute | solution.py:32
  87.6 17.6 %collective-permute-start.3 = (bf16[4,128,128]{2,1,0:T(8,128)(2,1)S(1)}, bf16[4,128,128]{2,1,0:T(8,128)(2,1)}, u32[]{:S(2)}, u32[]{:S(2)}) collective-permute-start(bf16[4,128,128]{2,1,0:T(8,128)(2,1)S(1)} %get-tuple-element.43), channel_id=1, source_target_pairs={{0,32},{8,40},{16,48},{24,56},{32,0},{40,8},{48,16},{56,24},{64,96... | collective-permute-start | bytes 393224 | tf_op jit(solution)/shard_map/ppermute | solution.py:32
  88.1 20.9 %collective-permute-start.4 = (bf16[4,128,128]{2,1,0:T(8,128)(2,1)S(1)}, bf16[4,128,128]{2,1,0:T(8,128)(2,1)}, u32[]{:S(2)}, u32[]{:S(2)}) collective-permute-start(bf16[4,128,128]{2,1,0:T(8,128)(2,1)S(1)} %get-tuple-element.43), channel_id=1, source_target_pairs={{0,40},{8,48},{16,56},{24,0},{32,8},{40,16},{48,24},{56,32},{64,10... | collective-permute-start | bytes 393224 | tf_op jit(solution)/shard_map/ppermute | solution.py:32
  95.3 15.9 %collective-permute-start.5 = (bf16[4,128,128]{2,1,0:T(8,128)(2,1)S(1)}, bf16[4,128,128]{2,1,0:T(8,128)(2,1)S(1)}, u32[]{:S(2)}, u32[]{:S(2)}) collective-permute-start(bf16[4,128,128]{2,1,0:T(8,128)(2,1)S(1)} %get-tuple-element.43), channel_id=1, source_target_pairs={{0,48},{8,56},{16,0},{24,8},{32,16},{40,24},{48,32},{56,40},{64,11... | collective-permute-start | bytes 393224 | tf_op jit(solution)/shard_map/ppermute | solution.py:32
  97.9 14.7 %collective-permute-start.6 = (bf16[4,128,128]{2,1,0:T(8,128)(2,1)S(1)}, bf16[4,128,128]{2,1,0:T(8,128)(2,1)S(1)}, u32[]{:S(2)}, u32[]{:S(2)}) collective-permute-start(bf16[4,128,128]{2,1,0:T(8,128)(2,1)S(1)} %get-tuple-element.43), channel_id=1, source_target_pairs={{0,56},{8,0},{16,8},{24,16},{32,24},{40,32},{48,40},{56,48},{64,12... | collective-permute-start | bytes 393224 | tf_op jit(solution)/shard_map/ppermute | solution.py:32
  113.7 8.6 %collective-permute-start.7 = (bf16[4,128,128]{2,1,0:T(8,128)(2,1)S(1)}, bf16[4,128,128]{2,1,0:T(8,128)(2,1)S(1)}, u32[]{:S(2)}, u32[]{:S(2)}) collective-permute-start(bf16[4,128,128]{2,1,0:T(8,128)(2,1)S(1)} %add_add_fusion), channel_id=1, source_target_pairs={{0,64},{8,72},{16,80},{24,88},{32,96},{40,104},{48,112},{56,120},{... | collective-permute-start | bytes 393224 | tf_op jit(solution)/shard_map/ppermute | solution.py:32
  115.4 7.6 %collective-permute-start.8 = (bf16[4,128,128]{2,1,0:T(8,128)(2,1)S(1)}, bf16[4,128,128]{2,1,0:T(8,128)(2,1)S(1)}, u32[]{:S(2)}, u32[]{:S(2)}) collective-permute-start(bf16[4,128,128]{2,1,0:T(8,128)(2,1)S(1)} %add_add_fusion), channel_id=1, source_target_pairs={{0,128},{8,136},{16,144},{24,152},{32,160},{40,168},{48,176},{56,1... | collective-permute-start | bytes 393224 | tf_op jit(solution)/shard_map/ppermute | solution.py:32
  116.3 7.4 %collective-permute-start.9 = (bf16[4,128,128]{2,1,0:T(8,128)(2,1)S(1)}, bf16[4,128,128]{2,1,0:T(8,128)(2,1)S(1)}, u32[]{:S(2)}, u32[]{:S(2)}) collective-permute-start(bf16[4,128,128]{2,1,0:T(8,128)(2,1)S(1)} %add_add_fusion), channel_id=1, source_target_pairs={{0,192},{8,200},{16,208},{24,216},{32,224},{40,232},{48,240},{56,2... | collective-permute-start | bytes 393224 | tf_op jit(solution)/shard_map/ppermute | solution.py:32
  121.6 3.3 %copy-start.1 = (f32[4,4,128,128]{3,2,1,0:T(8,128)S(1)}, f32[4,4,128,128]{3,2,1,0:T(8,128)}, u32[]{:S(2)}) copy-start(f32[4,4,128,128]{3,2,1,0:T(8,128)} %fusion.15) | copy-start | bytes 3145732
  124.4 1.2 copy-start.9
Sparse Core Ops, SparseCore 0:
  132.7 37.7 reduce-scatter.1
